TPU v7x, 256 devices: a whole 4x4x8 slice. The times are simulated.
256 devices in a mesh: tok: 64 (over z, x, core), wt: 4 (over y).
Axes of the slice: x: 4, y: 4, z: 8, core: 2. Of those that a mesh axis runs over, the one named last changes fastest.
Arguments:
- hidden_in: bfloat16 [15360, 5120], P('tok', 'wt'), may hold values from -6 to 6
- qkv_weight: bfloat16 [5120, 3584], P('tok', 'wt'), may hold values from -0.078125 to 0.078125
- qkv_bias: bfloat16 [3584], P('wt'), may hold values from -30 to 30
- page_pool: bfloat16 [192, 128, 1024], P('tok', None, 'wt'), may hold values from -36 to 36
- page_table: int32 [3, 50], replicated, may hold values from 0 to 191, as said below
- cached_lengths: int32 [3], replicated, may hold values from 1 to 1280
- token_request: int32 [15360], replicated, may hold values from 0 to 2, as said below
- token_position: int32 [15360], P('tok'), may hold values from 1 to 6399, as said below
Outputs:
- attended: bfloat16 [15360, 2560], P('tok', 'wt')
- new_pool: bfloat16 [192, 128, 1024], P('tok', None, 'wt')
Inputs may be any that keep to these rules, and one draw needn't show every extreme that they name: `page_table`: entries are distinct slots of the pool; the owner of slot g along tok is g div 3. `token_request`: new tokens come in 3 blocks of 5120, one request a block, in the order drawn. `token_position`: A request's new tokens have the consecutive positions cached_lengths[r] to cached_lengths[r] + 5119, in order.
All inputs are finite; a program needn't handle non-finite values.
Results may differ from a plain program's by a relative error of at most 0.0035.
The roundings to bfloat16 on the way count: a program that leaves them out, or rounds other values in their place, can miss the bound.
Values may be sent and summed in bfloat16 or wider, within the bound.
No kernel may reach another device: no remote copies, remote signals or barrier semaphores. Data moves between devices by JAX's collectives and lax.ppermute only.
A program may use at most 128 MiB of HBM per device.

v0:
```python
import math

import jax
import jax.numpy as jnp
from jax import lax
from jax.sharding import PartitionSpec as P

HEADS = 20
KVH = 4
HD = 128
PAGE = 128


ROPE_BASE = 1000000.0
NEG = -1e30


def rotate(part, positions):
    half = HD // 2
    freq = jnp.exp(jnp.arange(half, dtype=jnp.float32) * (-2.0 * math.log(ROPE_BASE) / HD))
    angle = positions.astype(jnp.float32)[:, None] * freq[None, :]
    cosine = jnp.cos(angle)[:, None, None, :]
    sine = jnp.sin(angle)[:, None, None, :]
    first = part[..., :half]
    second = part[..., half:]
    return jnp.concatenate([first * cosine - second * sine, second * cosine + first * sine], -1)


def finish(proj, positions):
    groups = proj.reshape(proj.shape[0], -1, HEADS // KVH + 2, HD)
    turned = rotate(groups[:, :, :-1], positions)
    queries = turned[:, :, :-1].astype(jnp.bfloat16)
    fresh = jnp.concatenate([turned[:, :, -1], groups[:, :, -1]], -1).astype(jnp.bfloat16)
    return (queries, fresh)


def attend(carry_state, queries, key_block, visible):
    maxima, totals, summed = carry_state
    keys = key_block[..., :HD]
    values = key_block[..., HD:]
    scores = jnp.einsum(
        "tgqd,kgd->gqtk", queries, keys, preferred_element_type=jnp.float32
    ) * HD ** (-0.5)
    shown = visible[None, None]
    peak = jnp.maximum(maxima, jnp.max(jnp.where(shown, scores, NEG), -1))
    probs = jnp.where(shown, jnp.exp(scores - peak[..., None]), 0.0)
    fade = jnp.exp(maxima - peak)
    totals = totals * fade + jnp.sum(probs, -1)
    summed = summed * fade[..., None] + jnp.einsum(
        "gqtk,kgd->gqtd", probs.astype(jnp.bfloat16), values, preferred_element_type=jnp.float32
    )
    return (peak, totals, summed)


def per_device(
    hidden_in,
    qkv_weight,
    qkv_bias,
    page_pool,
    page_table,
    cached_lengths,
    token_request,
    token_position,
):
    full_rows = lax.all_gather(hidden_in, "wt", axis=1, tiled=True)
    weight_all = lax.all_gather(qkv_weight, "tok", axis=0, tiled=True)
    proj = jnp.dot(full_rows, weight_all, preferred_element_type=jnp.float32)
    proj = proj + qkv_bias.astype(jnp.float32)
    queries, fresh = finish(proj, token_position)
    tok_dev = hidden_in.shape[0]
    local_groups = fresh.shape[1]
    kv_flat = fresh.reshape(tok_dev, local_groups * 2 * HD)
    total_tokens = token_request.shape[0]
    requests = cached_lengths.shape[0]
    new_len = total_tokens // requests
    cache_pages = (new_len // 4 + PAGE - 1) // PAGE
    pages_per = page_table.shape[1]
    slot_count = page_pool.shape[0]
    tok_index = lax.axis_index("tok")
    first_token = tok_index * tok_dev
    my_request = lax.dynamic_slice_in_dim(token_request, first_token, tok_dev)
    request_ids = jnp.arange(requests, dtype=jnp.int32)
    block_owner = token_request.reshape(requests, new_len)[:, 0]
    request_start = new_len * jnp.sum(
        (block_owner[None, :] == request_ids[:, None]) * request_ids[None, :], 1
    )
    token_ids = jnp.arange(total_tokens, dtype=jnp.int32)
    onehot = (token_request[:, None] == request_ids[None, :]).astype(jnp.int32)
    key_position = token_ids + jnp.sum(onehot * (cached_lengths - request_start)[None, :], 1)
    carry_state = (
        jnp.full((local_groups, HEADS // KVH, tok_dev), NEG, jnp.float32),
        jnp.zeros((local_groups, HEADS // KVH, tok_dev), jnp.float32),
        jnp.zeros((local_groups, HEADS // KVH, tok_dev, HD), jnp.float32),
    )
    cache_slots = page_table[:, :cache_pages].reshape(requests * cache_pages)
    local_slot = cache_slots - tok_index * slot_count
    owned = (local_slot >= 0) & (local_slot < slot_count)
    taken = jnp.take(page_pool, jnp.clip(local_slot, 0, slot_count - 1), axis=0)
    filled = jnp.where(owned[:, None, None], taken.astype(jnp.float32), 0.0)
    picked_all = lax.psum(filled, "tok").astype(jnp.bfloat16)
    cache_pos = jnp.arange(cache_pages * PAGE, dtype=jnp.int32)
    for request in range(requests):
        picked = picked_all[request * cache_pages : (request + 1) * cache_pages].reshape(
            cache_pages * PAGE, local_groups, 2 * HD
        )
        visible = (my_request == request)[:, None] & (cache_pos < cached_lengths[request])[None, :]

        def take_block(state_in, picked=picked, visible=visible):
            return attend(state_in, queries, picked, visible)

        def keep_block(state_in):
            return state_in

        carry_state = lax.cond(jnp.any(visible), take_block, keep_block, carry_state)
    kv_all = lax.all_gather(kv_flat, "tok", axis=0, tiled=True)
    row_floor = first_token // new_len * new_len
    row_span = min(total_tokens, new_len + tok_dev)
    row_count = kv_all.shape[0]
    block_width = min(row_count, max(512, -(-row_span // 16)))
    steps_count = -(-row_span // block_width)

    def one_block(block_index, state_now):
        wanted = row_floor - 0 + block_index * block_width
        offset = jnp.clip(wanted, 0, row_count - block_width)
        block_rows = lax.dynamic_slice_in_dim(kv_all, offset, block_width, 0).reshape(
            block_width, local_groups, 2 * HD
        )
        local_ids = offset + jnp.arange(block_width, dtype=jnp.int32)
        block_req = lax.dynamic_slice_in_dim(token_request, 0 + offset, block_width)
        block_pos = lax.dynamic_slice_in_dim(key_position, 0 + offset, block_width)
        visible = (
            (block_req[None, :] == my_request[:, None])
            & (block_pos[None, :] <= token_position[:, None])
            & (local_ids >= wanted)[None, :]
        )

        def take_block(state_use):
            return attend(state_use, queries, block_rows, visible)

        def keep_block(state_use):
            return state_use

        return lax.cond(jnp.any(visible), take_block, keep_block, state_now)

    carry_state = lax.fori_loop(0, steps_count, one_block, carry_state)
    pool_now = page_pool
    write_row_count = kv_all.shape[0]
    page_ids = jnp.arange(pages_per, dtype=jnp.int32)
    row_ids = jnp.arange(PAGE, dtype=jnp.int32)
    for slot_index in range(slot_count):
        global_slot = tok_index * slot_count + slot_index
        match = (page_table == global_slot).astype(jnp.int32)
        used = jnp.sum(match) > 0
        request = jnp.sum(match * request_ids[:, None])
        page_index = jnp.sum(match * page_ids[None, :])
        cached_here = jnp.sum(jnp.where(request_ids == request, cached_lengths, 0))
        start_here = jnp.sum(jnp.where(request_ids == request, request_start, 0))
        positions = page_index * PAGE + row_ids
        target = start_here + positions - cached_here
        valid = (
            used
            & (positions >= cached_here)
            & (positions < cached_here + new_len)
            & (target >= 0)
            & (target < 0 + write_row_count)
        )
        source = jnp.take(kv_all, jnp.clip(target - 0, 0, write_row_count - 1), axis=0)
        pool_now = pool_now.at[slot_index].set(
            jnp.where(valid[:, None], source, pool_now[slot_index])
        )
    maxima, totals, summed = carry_state
    attended = (
        (summed / totals[..., None])
        .transpose(2, 0, 1, 3)
        .reshape(tok_dev, local_groups * (HEADS // KVH) * HD)
        .astype(jnp.bfloat16)
    )
    return (attended, pool_now)


def solution(mesh):
    return jax.shard_map(
        per_device,
        mesh=mesh,
        in_specs=(
            P("tok", "wt"),
            P("tok", "wt"),
            P("wt"),
            P("tok", None, "wt"),
            P(),
            P(),
            P(),
            P("tok"),
        ),
        out_specs=(P("tok", "wt"), P("tok", None, "wt")),
        check_vma=False,
    )
```

profile of v0, /device:TPU:69, one launch (start us, length us, event | category | flops | bytes accessed | tf_op | source)
XLA Modules:
  0.0 559.1 jit_solution(15157018777026445762)
XLA Ops:
  10.9 37.3 %all-gather.4.cloned.1.call-done = bf16[240,5120]{1,0:T(8,128)(2,1)} async-done(((bf16[240,1280]{1,0:T(8,128)(2,1)}), bf16[240,5120]{1,0:T(8,128)(2,1)}) %all-gather.4.cloned.1.call-update) | async-done | bytes 2457616 | tf_op jit(solution)/shard_map/all_gather | solution.py:65
  48.2 84.6 %all-gather.6.cloned.1.call-done = bf16[5120,896]{1,0:T(8,128)(2,1)} async-done(((bf16[80,896]{1,0:T(8,128)(2,1)}), bf16[5120,896]{1,0:T(8,128)(2,1)}) %all-gather.6.cloned.1.call-update) | async-done | bytes 9175056 | tf_op jit(solution)/shard_map/all_gather | solution.py:66
  132.8 7.1 %convolution_add_fusion = f32[240,896]{1,0:T(8,128)S(1)} fusion(bf16[240,5120]{1,0:T(8,128)(2,1)} %all-gather.4.cloned.1.call-done, bf16[5120,896]{1,0:T(8,128)(2,1)} %all-gather.6.cloned.1.call-done, f32[896]{0:T(1024)S(1)} %convert_element_type.71), kind=kOutput, calls=%fused_computation.102 | convolution fusion | flops 2202224640 | bytes 12496384 | tf_op jit(solution)/shard_map/dot_general | solution.py:67
  151.4 2.9 convert_select_fusion
  173.0 267.3 %all-reduce.1 = bf16[30,128,256]{2,1,0:T(8,128)(2,1)S(1)} all-reduce(f32[30,128,256]{2,1,0:T(8,128)} %convert_select_fusion), channel_id=1, replica_groups=mesh['tok'=64,'wt'=4] {'tok'}, use_global_device_ids=true, to_apply=%region_3.4 | all-reduce | flops 983040 | bytes 5898240 | tf_op jit(solution)/shard_map/psum | solution.py:100
  442.5 8.2 %conditional.5 = ((f32[1,5,240]{2,1,0:T(8,128)S(1)}, f32[1,5,240]{2,1,0:T(8,128)S(1)}, f32[1,5,240,128]{3,2,1,0:T(8,128)})) conditional(s32[]{:T(128)} %convert_element_type.67, (f32[1,5,240]{2,1,0:T(8,128)S(1)}, f32[1,5,240]{2,1,0:T(8,128)S(1)}, f32[1,5,240,128]{3,2,1,0:T(8,128)}) %conditional.4, (pred[240,1280]{1,0:T(8,128)(4,1)S(1)}, ...), branch_computations={%region_8.9_spmd, %region_9.12_spmd} | conditional | flops 803638784 | bytes 24250044 | solution.py:114
  446.8 4.0 fusion.36
  450.8 7.2 %conditional.6 = ((f32[1,5,240]{2,1,0:T(8,128)S(1)}, f32[1,5,240]{2,1,0:T(8,128)S(1)}, f32[1,5,240,128]{3,2,1,0:T(8,128)})) conditional(s32[]{:T(128)} %convert_element_type.66, (f32[1,5,240]{2,1,0:T(8,128)S(1)}, f32[1,5,240]{2,1,0:T(8,128)S(1)}, f32[1,5,240,128]{3,2,1,0:T(8,128)}) %get-tuple-element.605, (pred[240,1280]{1,0:T(8,128)(4,1)S(1)}, ...), branch_computations={%region_12.13_spmd, %region_13.16_spmd} | conditional | flops 803638784 | bytes 22939296 | solution.py:114
  454.0 4.0 fusion.60
  458.0 76.1 %while.20 = (s32[]{:T(128)}, f32[1,5,240]{2,1,0:T(8,128)S(1)}, f32[1,5,240]{2,1,0:T(8,128)S(1)}, f32[1,5,240,128]{3,2,1,0:T(8,128)}, s32[]{:T(128)}, /*index=5*/...) while((s32[]{:T(128)}, f32[1,5,240]{2,1,0:T(8,128)S(1)}, ...), condition=%wide.region_24.25_spmd, body=%wide.region_18.24_spmd.sunk | while | flops 322257408 | bytes 10285903 | solution.py:145
  459.7 5.2 conditional.8
  466.7 5.2 conditional.8
  473.6 5.2 conditional.8
  480.5 5.2 conditional.8
  487.4 5.2 conditional.8
  494.3 5.2 conditional.8
  501.2 5.2 conditional.8
  508.1 5.2 conditional.8
  515.0 5.2 conditional.8
  522.0 5.2 conditional.8
  528.9 5.2 conditional.8
  536.5 5.0 gather_fusion.1
  541.6 5.0 gather_fusion.2
  546.8 5.0 gather_fusion.3
  (226 shorter events, 108.7 us)
Async XLA Ops:
  7.2 41.0 %all-gather.4.cloned.1.call-start = ((), (), s32[]{:S(2)}) async-start(), calls=%async_computation | async-start | bytes 3072000 | tf_op jit(solution)/shard_map/all_gather | solution.py:65
  8.1 143.1 %copy-start = (bf16[3,128,256]{2,1,0:T(8,128)(2,1)}, bf16[3,128,256]{2,1,0:T(8,128)(2,1)S(1)}, u32[]{:S(2)}) copy-start(bf16[3,128,256]{2,1,0:T(8,128)(2,1)S(1)} %copy.77) | copy-start | bytes 589828
  8.2 124.6 %all-gather.6.cloned.1.call-start = ((), (), s32[]{:S(2)}) async-start(), calls=%async_computation.1 | async-start | bytes 9318400 | tf_op jit(solution)/shard_map/all_gather | solution.py:66
  8.9 449.1 %all-gather.8.cloned.1.call-start = ((), (), s32[]{:S(2)}) async-start(), calls=%async_computation.2 | async-start | bytes 7987200 | tf_op jit(solution)/shard_map/all_gather | solution.py:115
  139.9 2.1 copy-start.9
  139.9 2.2 copy-start.7
  139.9 2.4 copy-start.10
  154.3 287.3 %copy-start.5 = (pred[240,1280]{1,0:T(8,128)(4,1)S(1)}, pred[240,1280]{1,0:T(8,128)(4,1)}, u32[]{:S(2)}) copy-start(pred[240,1280]{1,0:T(8,128)(4,1)} %get-tuple-element.437) | copy-start | bytes 921604
  441.6 1.0 copy-start.4
  442.5 8.2 %copy-start.3 = (pred[240,1280]{1,0:T(8,128)(4,1)S(1)}, pred[240,1280]{1,0:T(8,128)(4,1)}, u32[]{:S(2)}) copy-start(pred[240,1280]{1,0:T(8,128)(4,1)} %get-tuple-element.458) | copy-start | bytes 921604
  442.5 4.2 copy-start.6
  450.8 7.2 %copy-start.8 = (s32[240]{0:T(256)S(1)}, s32[240]{0:T(256)}, u32[]{:S(2)}) copy-start(s32[240]{0:T(256)} %param.33) | copy-start | bytes 2884
  458.0 83.5 %copy-start.1 = (bf16[3,128,256]{2,1,0:T(8,128)(2,1)S(1)}, bf16[3,128,256]{2,1,0:T(8,128)(2,1)}, u32[]{:S(2)}) copy-start(bf16[3,128,256]{2,1,0:T(8,128)(2,1)} %copy-done) | copy-start | bytes 589828
  458.0 83.5 %slice-start = ((bf16[3,128,256]{2,1,0:T(8,128)(2,1)}), bf16[1,128,256]{2,1,0:T(8,128)(2,1)S(1)}, s32[]{:S(2)}) async-start(bf16[3,128,256]{2,1,0:T(8,128)(2,1)} %copy-done), calls=%async_computation.3 | async-start | bytes 131072 | tf_op jit(solution)/shard_map/slice | solution.py:169
  458.0 83.5 %copy-start.11 = (pred[128]{0:T(512)(128)(4,1)S(1)}, pred[128]{0:T(512)(128)(4,1)}, u32[]{:S(2)}) copy-start(pred[128]{0:T(512)(128)(4,1)} %compare_and_fusion.5) | copy-start | bytes 388
  551.9 0.7 copy-start.2
Sparse Core Ops, SparseCore 0:
  9.8 38.3 all-gather.3
  50.9 81.8 all-gather.5
  142.0 79.7 all-gather.7
where the time goes:
time: 570 us; the launch traced here: 559 us
  blocking collectives  267 us (47%)
  waiting for transfers between devices  123 us (22%)
  matrix products  55.4 us (10%)
  other arithmetic  49.1 us (9%)
  local copies, waits for them, and re-layouts  35.3 us (6%)
  between operations  21.7 us (4%)
  loops' own time  7.45 us (1%)
    psum x1, blocking collectives, per_device(): picked_all = lax.psum(filled, 'tok').astype(jnp.bfloat16)  267 us
    all_gather x1, waiting for transfers between devices, per_device(): weight_all = lax.all_gather(qkv_weight, 'tok', axis=0, tiled=True)  84.6 us
    dot_general x13, matrix products, attend(): jnp.einsum('gqtk,kgd->gqtd', probs.astype(jnp.bfloat16), values, preferre...  37.5 us
    all_gather x1, waiting for transfers between devices, per_device(): full_rows = lax.all_gather(hidden_in, 'wt', axis=1, tiled=True)  37.3 us
    gather x3, local copies, waits for them, and re-layouts, per_device(): jnp.take(kv_all, jnp.clip(target - 0, 0, write_row_count - 1), axis=0)  15 us
    reduce_sum x13, other arithmetic, attend(): totals = totals * fade + jnp.sum(probs, -1)  12.7 us
  transfers between devices with their start and end apart: 3, of which 2 were waited for; matrix products, arithmetic and copies ran while one was open for 8% of the time, Pallas kernels for 0%

commit v1 on v0

v1 whole, which is shorter than its diff:
```python
import math

import jax
import jax.numpy as jnp
from jax import lax
from jax.experimental import pallas as pl
from jax.experimental.pallas import tpu as pltpu
from jax.sharding import PartitionSpec as P

HEADS = 20
KVH = 4
HD = 128
PAGE = 128


ROPE_BASE = 1000000.0
NEG = -1e30


def rotate(part, positions):
    half = HD // 2
    freq = jnp.exp(jnp.arange(half, dtype=jnp.float32) * (-2.0 * math.log(ROPE_BASE) / HD))
    angle = positions.astype(jnp.float32)[:, None] * freq[None, :]
    cosine = jnp.cos(angle)[:, None, None, :]
    sine = jnp.sin(angle)[:, None, None, :]
    first = part[..., :half]
    second = part[..., half:]
    return jnp.concatenate([first * cosine - second * sine, second * cosine + first * sine], -1)


def finish(proj, positions):
    groups = proj.reshape(proj.shape[0], -1, HEADS // KVH + 2, HD)
    turned = rotate(groups[:, :, :-1], positions)
    queries = turned[:, :, :-1].astype(jnp.bfloat16)
    fresh = jnp.concatenate([turned[:, :, -1], groups[:, :, -1]], -1).astype(jnp.bfloat16)
    return (queries, fresh)

def flash_body(off_ref, flag_ref, q_ref, qpos_ref, qreq_ref, kv_ref, kpos_ref, kreq_ref,
               m_in, l_in, acc_in, m_out, l_out, acc_out):
    j = pl.program_id(0)

    @pl.when(j == 0)
    def _():
        m_out[...] = m_in[...]
        l_out[...] = l_in[...]
        acc_out[...] = acc_in[...]

    @pl.when(flag_ref[j] > 0)
    def _():
        kv = kv_ref[...]
        keys = kv[:, :HD]
        values = kv[:, HD:]
        scores = lax.dot_general(q_ref[...], keys, (((1,), (1,)), ((), ())),
                                 preferred_element_type=jnp.float32) * HD ** (-0.5)
        shown = (kreq_ref[...] == qreq_ref[...]) & (kpos_ref[...] <= qpos_ref[...])
        maxima = m_out[...]
        peak = jnp.maximum(maxima, jnp.max(jnp.where(shown, scores, NEG), axis=1, keepdims=True))
        probs = jnp.where(shown, jnp.exp(scores - peak), 0.0)
        fade = jnp.exp(maxima - peak)
        l_out[...] = l_out[...] * fade + jnp.sum(probs, axis=1, keepdims=True)
        acc_out[...] = acc_out[...] * fade + jnp.dot(
            probs.astype(jnp.bfloat16), values, preferred_element_type=jnp.float32)
        m_out[...] = peak


def flash_part(state, q, qpos, qreq, kv, kpos, kreq, first_block, flags, block):
    maxima, totals, summed = state
    rows = q.shape[0]
    nb = kv.shape[0] // block
    steps = flags.shape[0]

    def kv_map(j, off, fl):
        return (jnp.minimum(off[0] + j, nb - 1), 0)

    def k_map(j, off, fl):
        return (0, jnp.minimum(off[0] + j, nb - 1))

    def whole(j, off, fl):
        return (0, 0)

    grid_spec = pltpu.PrefetchScalarGridSpec(
        num_scalar_prefetch=2,
        grid=(steps,),
        in_specs=[
            pl.BlockSpec((rows, HD), whole),
            pl.BlockSpec((rows, 1), whole),
            pl.BlockSpec((rows, 1), whole),
            pl.BlockSpec((block, 2 * HD), kv_map),
            pl.BlockSpec((1, block), k_map),
            pl.BlockSpec((1, block), k_map),
            pl.BlockSpec((rows, 1), whole),
            pl.BlockSpec((rows, 1), whole),
            pl.BlockSpec((rows, HD), whole),
        ],
        out_specs=[
            pl.BlockSpec((rows, 1), whole),
            pl.BlockSpec((rows, 1), whole),
            pl.BlockSpec((rows, HD), whole),
        ],
    )
    return pl.pallas_call(
        flash_body,
        grid_spec=grid_spec,
        out_shape=[
            jax.ShapeDtypeStruct((rows, 1), jnp.float32),
            jax.ShapeDtypeStruct((rows, 1), jnp.float32),
            jax.ShapeDtypeStruct((rows, HD), jnp.float32),
        ],
        compiler_params=pltpu.CompilerParams(dimension_semantics=("arbitrary",)),
    )(first_block.reshape(1), flags, q, qpos, qreq, kv, kpos.reshape(1, -1), kreq.reshape(1, -1),
      maxima, totals, summed)


def per_device(
    hidden_in,
    qkv_weight,
    qkv_bias,
    page_pool,
    page_table,
    cached_lengths,
    token_request,
    token_position,
):
    wt_count = 4
    wt_index = lax.axis_index("wt")
    pieces = [hidden_in] + [
        lax.ppermute(hidden_in, "wt", [(i, (i + k) % wt_count) for i in range(wt_count)])
        for k in range(1, wt_count)
    ]
    order = (wt_index - jnp.arange(wt_count, dtype=jnp.int32)) % wt_count
    stacked = jnp.take(jnp.stack(pieces, 0), order, axis=0)
    full_rows = jnp.transpose(stacked, (1, 0, 2)).reshape(hidden_in.shape[0], -1)
    weight_all = lax.all_gather(qkv_weight, "tok", axis=0, tiled=True)
    proj = jnp.dot(full_rows, weight_all, preferred_element_type=jnp.float32)
    proj = proj + qkv_bias.astype(jnp.float32)
    queries, fresh = finish(proj, token_position)
    tok_dev = hidden_in.shape[0]
    local_groups = fresh.shape[1]
    kv_flat = fresh.reshape(tok_dev, local_groups * 2 * HD)
    total_tokens = token_request.shape[0]
    requests = cached_lengths.shape[0]
    new_len = total_tokens // requests
    cache_pages = (new_len // 4 + PAGE - 1) // PAGE
    pages_per = page_table.shape[1]
    slot_count = page_pool.shape[0]
    tok_index = lax.axis_index("tok")
    first_token = tok_index * tok_dev
    my_request = lax.dynamic_slice_in_dim(token_request, first_token, tok_dev)
    request_ids = jnp.arange(requests, dtype=jnp.int32)
    block_owner = token_request.reshape(requests, new_len)[:, 0]
    request_start = new_len * jnp.sum(
        (block_owner[None, :] == request_ids[:, None]) * request_ids[None, :], 1
    )
    token_ids = jnp.arange(total_tokens, dtype=jnp.int32)
    onehot = (token_request[:, None] == request_ids[None, :]).astype(jnp.int32)
    key_position = token_ids + jnp.sum(onehot * (cached_lengths - request_start)[None, :], 1)
    cache_slots = page_table[:, :cache_pages].reshape(requests * cache_pages)
    kv_all = lax.all_gather(kv_flat, "tok", axis=0, tiled=True)
    kv_all, pool_src = lax.optimization_barrier((kv_all, page_pool))
    row_floor = first_token // new_len * new_len
    row_span = min(total_tokens, new_len + tok_dev)
    heads_per = HEADS // KVH
    q_rows = jnp.transpose(queries, (1, 2, 0, 3)).reshape(local_groups * heads_per * tok_dev, HD)
    qpos_rows = jnp.tile(token_position, local_groups * heads_per).reshape(-1, 1)
    qreq_rows = jnp.tile(my_request, local_groups * heads_per).reshape(-1, 1)
    state = (
        jnp.full((q_rows.shape[0], 1), NEG, jnp.float32),
        jnp.zeros((q_rows.shape[0], 1), jnp.float32),
        jnp.zeros((q_rows.shape[0], HD), jnp.float32),
    )
    req_max = jnp.max(
        jnp.where(my_request[None, :] == request_ids[:, None], token_position[None, :], -1), axis=1
    )
    fresh_block = 512
    fresh_steps = -(-row_span // fresh_block)
    first_fresh = row_floor // fresh_block
    intended = (first_fresh + jnp.arange(fresh_steps, dtype=jnp.int32))[:, None] * fresh_block + jnp.arange(
        fresh_block, dtype=jnp.int32
    )[None, :]
    inside = intended < total_tokens
    rows_in = jnp.clip(intended, 0, total_tokens - 1)
    seen = inside & (
        jnp.take(key_position, rows_in) <= jnp.take(req_max, jnp.take(token_request, rows_in))
    )
    fresh_flags = jnp.any(seen, axis=1).astype(jnp.int32)
    state = flash_part(
        state, q_rows, qpos_rows, qreq_rows, kv_all, key_position, token_request,
        first_fresh.astype(jnp.int32), fresh_flags, fresh_block,
    )
    pool_all = lax.all_gather(pool_src, "tok", axis=0, tiled=True)
    cache_slots = page_table[:, :cache_pages].reshape(requests * cache_pages)
    picked_rows = jnp.take(pool_all, cache_slots, axis=0).reshape(requests * cache_pages * PAGE, -1)
    cache_ids = jnp.arange(requests * cache_pages * PAGE, dtype=jnp.int32)
    cache_req = cache_ids // (cache_pages * PAGE)
    cache_in = cache_ids % (cache_pages * PAGE)
    cache_pos = jnp.where(cache_in < jnp.take(cached_lengths, cache_req), cache_in, 1 << 30)
    cache_block = 5 * PAGE
    cache_steps = cache_ids.shape[0] // cache_block
    cache_flags = jnp.any(
        (cache_pos <= jnp.take(req_max, cache_req)).reshape(cache_steps, cache_block), axis=1
    ).astype(jnp.int32)
    state = flash_part(
        state, q_rows, qpos_rows, qreq_rows, picked_rows, cache_pos, cache_req,
        jnp.zeros((), jnp.int32), cache_flags, cache_block,
    )
    pool_now = page_pool
    write_row_count = kv_all.shape[0]
    page_ids = jnp.arange(pages_per, dtype=jnp.int32)
    row_ids = jnp.arange(PAGE, dtype=jnp.int32)
    for slot_index in range(slot_count):
        global_slot = tok_index * slot_count + slot_index
        match = (page_table == global_slot).astype(jnp.int32)
        used = jnp.sum(match) > 0
        request = jnp.sum(match * request_ids[:, None])
        page_index = jnp.sum(match * page_ids[None, :])
        cached_here = jnp.sum(jnp.where(request_ids == request, cached_lengths, 0))
        start_here = jnp.sum(jnp.where(request_ids == request, request_start, 0))
        positions = page_index * PAGE + row_ids
        target = start_here + positions - cached_here
        valid = (
            used
            & (positions >= cached_here)
            & (positions < cached_here + new_len)
            & (target >= 0)
            & (target < 0 + write_row_count)
        )
        source = jnp.take(kv_all, jnp.clip(target - 0, 0, write_row_count - 1), axis=0)
        pool_now = pool_now.at[slot_index].set(
            jnp.where(valid[:, None], source, pool_now[slot_index])
        )
    maxima, totals, summed = state
    attended = (
        (summed / totals)
        .reshape(local_groups, heads_per, tok_dev, HD)
        .transpose(2, 0, 1, 3)
        .reshape(tok_dev, local_groups * heads_per * HD)
        .astype(jnp.bfloat16)
    )
    return (attended, pool_now)


def solution(mesh):
    return jax.shard_map(
        per_device,
        mesh=mesh,
        in_specs=(
            P("tok", "wt"),
            P("tok", "wt"),
            P("wt"),
            P("tok", None, "wt"),
            P(),
            P(),
            P(),
            P("tok"),
        ),
        out_specs=(P("tok", "wt"), P("tok", None, "wt")),
        check_vma=False,
    )
```

time: 570 us -> 390 us (0.68); the launches traced: 559 us -> 387 us
  blocking collectives: 267 us -> 0 us
  local copies, waits for them, and re-layouts: 35.3 us -> 126 us
  matrix products: 55.4 us -> 6.31 us
  Pallas kernels: 0 us -> 45 us
  waiting for transfers between devices: 123 us -> 152 us
  other arithmetic: 49.1 us -> 33.7 us
  loops' own time: 7.45 us -> 0 us
    psum x1 -> x0, blocking collectives: 267 us -> none  [per_device(): picked_all = lax.psum(filled, 'tok').astype(jnp.bfloat16)]
    gather x1 -> x10, local copies, waits for them, and re-layouts: 0.67 us -> 99.3 us  [the longest x2 31.7 us: per_device(): jnp.take(req_max, jnp.take(token_request, rows_in))]
    all_gather x1, waiting for transfers between devices: 0.01 us -> 79 us  [per_device(): kv_all = lax.all_gather(kv_flat, 'tok', axis=0, tiled=True)]
    dot_general x26 -> x0, matrix products: 48.3 us -> none  [the longest x13 37.5 us: attend(): jnp.einsum('gqtk,kgd->gqtd', probs.astype(jnp.bfloat16), values, preferre...]
    pallas_call x0 -> x2, Pallas kernels: none -> 45 us  [flash_part(): pl.pallas_call(flash_body, grid_spec=grid_spec, out_shape=[jax.ShapeDtype...]
    all_gather x1, waiting for transfers between devices: 84.6 us -> 46.3 us  [per_device(): weight_all = lax.all_gather(qkv_weight, 'tok', axis=0, tiled=True)]
    all_gather x1, waiting for transfers between devices: 37.3 us -> 0.01 us  [per_device(): pool_all = lax.all_gather(pool_src, 'tok', axis=0, tiled=True)]
    ppermute x0 -> x3, waiting for transfers between devices: none -> 27 us  [per_device(): lax.ppermute(hidden_in, 'wt', [(i, (i + k) % wt_count) for i in range(wt_...]
  transfers between devices with their start and end apart: 3 -> 6, of which waited for: 2 -> 5; matrix products, arithmetic and copies ran while one was open for 8% -> 37% of each run, Pallas kernels for 0% -> 7%
where the time goes in v1:
time: 390 us; the launch traced here: 387 us
  waiting for transfers between devices  152 us (39%)
  local copies, waits for them, and re-layouts  126 us (32%)
  Pallas kernels  45 us (12%)
  other arithmetic  33.7 us (9%)
  between operations  19.8 us (5%)
  matrix products  6.31 us (2%)
  starting transfers between devices  4.15 us (1%)
    all_gather x1, waiting for transfers between devices, per_device(): kv_all = lax.all_gather(kv_flat, 'tok', axis=0, tiled=True)  79 us
    all_gather x1, waiting for transfers between devices, per_device(): weight_all = lax.all_gather(qkv_weight, 'tok', axis=0, tiled=True)  46.3 us
    pallas_call x2, Pallas kernels, flash_part(): pl.pallas_call(flash_body, grid_spec=grid_spec, out_shape=[jax.ShapeDtype...  45 us
    gather x2, local copies, waits for them, and re-layouts, per_device(): jnp.take(req_max, jnp.take(token_request, rows_in))  31.7 us
    gather x2, local copies, waits for them, and re-layouts, per_device(): jnp.take(key_position, rows_in)  29.3 us
    gather x2, local copies, waits for them, and re-layouts, per_device(): jnp.take(token_request, rows_in)  29.3 us
    ppermute x3, waiting for transfers between devices, per_device(): lax.ppermute(hidden_in, 'wt', [(i, (i + k) % wt_count) for i in range(wt_...  27 us
    gather x3, local copies, waits for them, and re-layouts, per_device(): jnp.take(kv_all, jnp.clip(target - 0, 0, write_row_count - 1), axis=0)  15 us
  transfers between devices with their start and end apart: 6, of which 5 were waited for; matrix products, arithmetic and copies ran while one was open for 37% of the time, Pallas kernels for 7%

profile of v1, /device:TPU:69, one launch (start us, length us, event | category | flops | bytes accessed | tf_op | source)
XLA Modules:
  0.0 387.2 jit_solution(15730319409603301234)
XLA Ops:
  8.9 2.8 collective-permute-start.2
  15.3 10.2 %collective-permute-done.2 = bf16[240,1280]{1,0:T(8,128)(2,1)S(1)} collective-permute-done((bf16[240,1280]{1,0:T(8,128)(2,1)}, bf16[240,1280]{1,0:T(8,128)(2,1)S(1)}, u32[]{:S(2)}, u32[]{:S(2)}) %collective-permute-start.2) | collective-permute-done | bytes 614432 | tf_op jit(solution)/shard_map/ppermute | solution.py:127
  25.6 2.4 collective-permute-done.1
  27.9 14.4 %collective-permute-done = bf16[240,1280]{1,0:T(8,128)(2,1)S(1)} collective-permute-done((bf16[240,1280]{1,0:T(8,128)(2,1)}, bf16[240,1280]{1,0:T(8,128)(2,1)S(1)}, u32[]{:S(2)}, u32[]{:S(2)}) %collective-permute-start) | collective-permute-done | bytes 614432 | tf_op jit(solution)/shard_map/ppermute | solution.py:127
  42.4 2.8 pad_maximum_fusion
  45.2 2.4 gather_fusion
  48.2 46.3 %all-gather.4.cloned.1.call-done = bf16[5120,896]{1,0:T(8,128)(2,1)} async-done(((bf16[80,896]{1,0:T(8,128)(2,1)}), bf16[5120,896]{1,0:T(8,128)(2,1)}) %all-gather.4.cloned.1.call-update) | async-done | bytes 9175056 | tf_op jit(solution)/shard_map/all_gather | solution.py:133
  94.5 6.3 %convolution_add_fusion = f32[240,896]{1,0:T(8,128)S(1)} fusion(bf16[240,5120]{1,0:T(8,128)(2,1)S(1)} %bitcast.76, bf16[5120,896]{1,0:T(8,128)(2,1)} %all-gather.4.cloned.1.call-done, f32[896]{0:T(1024)S(1)} %convert_element_type.41), kind=kOutput, calls=%fused_computation.11 | convolution fusion | flops 2202224640 | bytes 12496384 | tf_op jit(solution)/shard_map/dot_general | solution.py:134
  103.3 79.0 %all-gather.6.cloned.1.call-done.kv_ref = bf16[15360,256]{1,0:T(8,128)(2,1)} async-done(((bf16[240,256]{1,0:T(8,128)(2,1)}), bf16[15360,256]{1,0:T(8,128)(2,1)}) %all-gather.6.cloned.1.call-update) | async-done | bytes 7864336 | tf_op jit(solution)/shard_map/all_gather | solution.py:158
  184.1 3.8 select_compare_fusion.1
  193.5 29.3 %gather_fusion.4 = s32[5632]{0:T(1024)S(1)} fusion(s32[15360]{0:T(1024)S(1)} %copy-done, s32[6144]{0:T(1024)S(1)} %pad_clamp_fusion.1), kind=kCustom, calls=%fused_computation.2.clone | custom fusion | bytes 67584 | tf_op jit(solution)/shard_map/jit(_take)/gather | solution.py:183
  222.9 31.7 %gather_fusion.2 = s32[5632]{0:T(1024)S(1)} fusion(s32[3]{0:T(128)S(1)} %select_reduce_fusion.1, s32[6144]{0:T(1024)S(1)} %pad_clamp_fusion), kind=kCustom, calls=%fused_computation.7 | custom fusion | bytes 67584 | tf_op jit(solution)/shard_map/jit(_take)/gather | solution.py:183
  257.0 2.5 fusion.20
  259.8 29.3 %gather_fusion.3 = s32[5632]{0:T(1024)S(1)} fusion(s32[15360]{0:T(1024)S(1)} %iota_add_fusion.1, s32[6144]{0:T(1024)S(1)} %pad_clamp_fusion.1), kind=kCustom, calls=%fused_computation.clone | custom fusion | bytes 67584 | tf_op jit(solution)/shard_map/jit(_take)/gather | solution.py:183
  295.5 2.4 compare_and_fusion.6
  297.9 2.4 compare_and_fusion.4
  300.3 2.4 compare_and_fusion.2
  305.1 5.0 %gather_fusion.5 = bf16[128,256]{1,0:T(8,128)(2,1)S(1)} fusion(bf16[15360,256]{1,0:T(8,128)(2,1)} %all-gather.6.cloned.1.call-done.kv_ref, s32[1024]{0:T(1024)S(1)} %pad_clamp_fusion.4), kind=kCustom, calls=%fused_computation.1.clone | custom fusion | bytes 131584 | tf_op jit(solution)/shard_map/jit(_take)/gather | solution.py:227
  310.1 5.0 %gather_fusion.6 = bf16[128,256]{1,0:T(8,128)(2,1)S(1)} fusion(bf16[15360,256]{1,0:T(8,128)(2,1)} %all-gather.6.cloned.1.call-done.kv_ref, s32[1024]{0:T(1024)S(1)} %pad_clamp_fusion.3), kind=kCustom, calls=%fused_computation.3.clone | custom fusion | bytes 131584 | tf_op jit(solution)/shard_map/jit(_take)/gather | solution.py:227
  315.1 5.0 %gather_fusion.7 = bf16[128,256]{1,0:T(8,128)(2,1)S(1)} fusion(bf16[15360,256]{1,0:T(8,128)(2,1)} %all-gather.6.cloned.1.call-done.kv_ref, s32[1024]{0:T(1024)S(1)} %pad_clamp_fusion.2), kind=kCustom, calls=%fused_computation.4.clone | custom fusion | bytes 131584 | tf_op jit(solution)/shard_map/jit(_take)/gather | solution.py:227
  322.8 27.7 %shard_map.95 = (f32[1200,1]{1,0:T(8,128)}, f32[1200,1]{1,0:T(8,128)}, f32[1200,128]{1,0:T(8,128)}) custom-call(s32[1]{0:T(128)} %bitcast.20.off_ref, s32[11]{0:T(128)} %convert_element_type.43.flag_ref, bf16[1200,128]{1,0:T(8,128)(2,1)} %bitcast.74, s32[1200,1]{1,0:T(8,128)} %reshape_tile.8.qpos_ref, s32[1200,1]{1,0:T(8,128)} %reshape_tile.9.qreq_ref, ...), custom_call_target="tpu_custom_call" | custom-call | tf_op jit(solution)/shard_map/pallas_call | solution.py:101
  350.5 5.2 %gather_fusion.1 = bf16[30,128,256]{2,1,0:T(8,128)(2,1)S(1)} fusion(bf16[192,128,256]{2,1,0:T(8,128)(2,1)} %all-gather.8.cloned.1.call-done, s32[1024]{0:T(1024)S(1)} %pad_clamp_fusion.5), kind=kCustom, calls=%fused_computation.6 | custom fusion | bytes 3932280 | tf_op jit(solution)/shard_map/jit(_take)/gather | solution.py:192
  355.7 2.9 bitcast_select_fusion.kv_ref
  358.6 17.3 %shard_map.96 = (f32[1200,1]{1,0:T(8,128)}, f32[1200,1]{1,0:T(8,128)}, f32[1200,128]{1,0:T(8,128)}) custom-call(s32[1]{0:T(128)} %constant.227.clone.1.off_ref, s32[6]{0:T(128)} %convert_element_type.40.flag_ref, bf16[1200,128]{1,0:T(8,128)(2,1)} %bitcast.75, s32[1200,1]{1,0:T(8,128)} %reshape_tile.8.qpos_ref, s32[1200,1]{1,0:T(8,128)} %reshape_tile.9.qreq_ref, ...), custom_call_target="tpu_custom_call" | custom-call | tf_op jit(solution)/shard_map/pallas_call | solution.py:101
  (100 shorter events, 28.7 us)
Async XLA Ops:
  7.2 87.4 %all-gather.4.cloned.1.call-start = ((), (), s32[]{:S(2)}) async-start(), calls=%async_computation | async-start | bytes 9318400 | tf_op jit(solution)/shard_map/all_gather | solution.py:133
  8.9 173.4 %all-gather.6.cloned.1.call-start = ((), (), s32[]{:S(2)}) async-start(), calls=%async_computation.1 | async-start | bytes 7987200 | tf_op jit(solution)/shard_map/all_gather | solution.py:158
  8.9 16.7 %collective-permute-start.2 = (bf16[240,1280]{1,0:T(8,128)(2,1)}, bf16[240,1280]{1,0:T(8,128)(2,1)S(1)}, u32[]{:S(2)}, u32[]{:S(2)}) collective-permute-start(bf16[240,1280]{1,0:T(8,128)(2,1)} %param.20), channel_id=1, source_target_pairs={{0,3},{1,0},{2,1},{3,2},{4,7},{5,4},{6,5},{7,6},{8,11},{9,8},{10,9... | collective-permute-start | bytes 1843208 | tf_op jit(solution)/shard_map/ppermute | solution.py:127
  11.7 16.2 %collective-permute-start.1 = (bf16[240,1280]{1,0:T(8,128)(2,1)}, bf16[240,1280]{1,0:T(8,128)(2,1)S(1)}, u32[]{:S(2)}, u32[]{:S(2)}) collective-permute-start(bf16[240,1280]{1,0:T(8,128)(2,1)} %param.20), channel_id=1, source_target_pairs={{0,2},{1,3},{2,0},{3,1},{4,6},{5,7},{6,4},{7,5},{8,10},{9,11},{10,... | collective-permute-start | bytes 1843208 | tf_op jit(solution)/shard_map/ppermute | solution.py:127
  12.1 30.3 %collective-permute-start = (bf16[240,1280]{1,0:T(8,128)(2,1)}, bf16[240,1280]{1,0:T(8,128)(2,1)S(1)}, u32[]{:S(2)}, u32[]{:S(2)}) collective-permute-start(bf16[240,1280]{1,0:T(8,128)(2,1)} %param.20), channel_id=1, source_target_pairs={{0,1},{1,2},{2,3},{3,0},{4,5},{5,6},{6,7},{7,4},{8,9},{9,10},{10,1... | collective-permute-start | bytes 1843208 | tf_op jit(solution)/shard_map/ppermute | solution.py:127
  101.1 0.9 copy-start.3
  101.5 80.8 %copy-start.4 = (s32[3,50]{1,0:T(4,128)S(1)}, s32[3,50]{1,0:T(4,128)}, u32[]{:S(2)}) copy-start(s32[3,50]{1,0:T(4,128)} %param.24) | copy-start | bytes 1804
  101.5 81.0 %copy-start.1 = (bf16[3,128,256]{2,1,0:T(8,128)(2,1)S(1)}, bf16[3,128,256]{2,1,0:T(8,128)(2,1)}, u32[]{:S(2)}) copy-start(bf16[3,128,256]{2,1,0:T(8,128)(2,1)} %copy.63) | copy-start | bytes 589828
  101.5 80.9 %copy-start = (s32[15360]{0:T(1024)S(1)}, s32[15360]{0:T(1024)}, u32[]{:S(2)}) copy-start(s32[15360]{0:T(1024)} %param.26) | copy-start | bytes 184324
  101.5 81.1 %copy-start.5 = (s32[240]{0:T(256)S(1)}, s32[240]{0:T(256)}, u32[]{:S(2)}) copy-start(s32[240]{0:T(256)} %param.27) | copy-start | bytes 2884
  101.6 81.8 %copy-start.6 = (s32[3]{0:T(128)S(1)}, s32[3]{0:T(128)}, u32[]{:S(2)}) copy-start(s32[3]{0:T(128)} %param.25) | copy-start | bytes 40
  103.0 247.4 %all-gather.8.cloned.1.call-start = ((), (), s32[]{:S(2)}) async-start(), calls=%async_computation.2 | async-start | bytes 12779520 | tf_op jit(solution)/shard_map/all_gather | solution.py:190
  380.0 0.7 copy-start.2
Sparse Core Ops, SparseCore 0:
  10.7 83.8 all-gather.3
  103.2 79.0 all-gather.5
  185.6 86.8 all-gather.7
